TPU v7x, 256 devices: a whole 4x4x8 slice. The times are simulated.
256 devices in a mesh: grp: 8 (over x, core), dev: 32 (over z, y).
Axes of the slice: x: 4, y: 4, z: 8, core: 2. Of those that a mesh axis runs over, the one named last changes fastest.
Arguments:
- references: bfloat16 [192, 2048], P('dev'), may hold values from -4 to 4
- particles: bfloat16 [2048, 65536], P(None, ('grp', 'dev')), may hold values from -1300 to 1300
- defocus_bin: int32 [65536], P(('grp', 'dev')), may hold values from 0 to 63
- contrast_table: float32 [64, 32], replicated, may hold values from 0.1 to 1
- noise_power: float32 [32], replicated, may hold values from 300 to 3000
- class_prior: float32 [192], replicated, may hold values from -3 to 3
Outputs:
- new_references: float32 [192, 2048], P('dev')
- occupancy: float32 [192], P('dev')
All inputs are finite; a program needn't handle non-finite values.
Results may differ from a plain program's by a relative error of at most 0.0015.
Values may be sent and summed in bfloat16 or wider, within the bound.
No kernel may reach another device: no remote copies, remote signals or barrier semaphores. Data moves between devices by JAX's collectives and lax.ppermute only.
A program may use at most 64 MiB of HBM per device.

v0:
```python
import math
import jax
import jax.numpy as jnp
from jax import lax
from jax.sharding import PartitionSpec as P

Q = 32
M = 32
R = 128
CLS_DEV = 6


def angle_tables(cycle_freqs, count_turns):
    freq_index = jnp.arange(cycle_freqs, dtype=jnp.int32)
    turn_index = jnp.arange(count_turns, dtype=jnp.int32)
    wrapped = freq_index[:, None] * turn_index[None, :] % count_turns
    phases = 2.0 * math.pi / count_turns * wrapped.astype(jnp.float32)
    factor = jnp.where(freq_index == 0, 1.0, 2.0).astype(jnp.float32)[:, None]
    cosine = jnp.cos(phases)
    sine_part = jnp.sin(phases)
    score_table = jnp.stack([factor * cosine, factor * sine_part], 0).astype(jnp.bfloat16)
    turn_table = jnp.stack([cosine, sine_part], 0).astype(jnp.bfloat16)
    return (score_table, turn_table)


def particle_terms(particles, defocus_bin, contrast_table, noise_power):
    columns = particles.shape[1]
    cycle_count = contrast_table.shape[1]
    freq_count = particles.shape[0] // (2 * cycle_count)
    onehot = (
        defocus_bin[None, :] == jnp.arange(contrast_table.shape[0], dtype=jnp.int32)[:, None]
    ).astype(jnp.float32)
    contrast = jnp.dot(contrast_table.T, onehot, precision=lax.Precision.HIGHEST)
    scaled = contrast / noise_power[:, None]
    power_term = contrast * scaled
    weighted = (
        particles.astype(jnp.float32).reshape(freq_count, 2, cycle_count, columns)
        * scaled[None, None]
    ).astype(jnp.bfloat16)
    return (weighted.reshape(freq_count, 2 * cycle_count, columns), power_term)


def class_rows(class_block):
    classes = class_block.shape[0]
    class_grid = class_block.reshape(classes, M, 2, Q)
    real_part = class_grid[:, :, 0, :]
    imag_part = class_grid[:, :, 1, :]
    rows_real = jnp.concatenate([real_part, imag_part], -1)
    rows_imag = jnp.concatenate([-imag_part, real_part], -1)
    stacked = jnp.stack([rows_real, rows_imag], 0)
    factor = jnp.where(jnp.arange(M) == 0, 1.0, 2.0).astype(jnp.float32)
    squares = class_grid.astype(jnp.float32) ** 2
    cycle_power = jnp.sum(jnp.sum(squares, axis=2) * factor[None, :, None], axis=1)
    return (stacked, cycle_power)


def block_rows(total_rows):
    return CLS_DEV * math.gcd(total_rows // CLS_DEV, 4)


def local(references, particles, defocus_bin, contrast_table, noise_power, class_prior):
    weighted, power_term = particle_terms(particles, defocus_bin, contrast_table, noise_power)
    score_table, turn_table = angle_tables(M, R)
    columns = particles.shape[1]
    classes_total = CLS_DEV * lax.axis_size("dev")

    def block_scores(class_block, first_row):
        stacked, cycle_power = class_rows(class_block)
        prior_part = lax.dynamic_slice_in_dim(class_prior, first_row, class_block.shape[0], 0)
        crossed = jnp.einsum(
            "pkmc,mcb->pmkb", stacked, weighted, preferred_element_type=jnp.float32
        ).astype(jnp.bfloat16)
        scores = jnp.einsum(
            "pmkb,pmr->krb", crossed, score_table, preferred_element_type=jnp.float32
        )
        penalty = jnp.dot(cycle_power, power_term, precision=lax.Precision.HIGHEST)
        return scores - 0.5 * penalty[:, None, :] + prior_part[:, None, None]

    initial = (jnp.full((columns,), -1e30, jnp.float32), jnp.zeros((columns,), jnp.float32))
    empty_sums = (
        jnp.zeros((classes_total, 2 * M * Q), jnp.float32),
        jnp.zeros((classes_total, Q), jnp.float32),
        jnp.zeros((classes_total,), jnp.float32),
    )
    gathered = lax.all_gather(references, "dev", axis=0, tiled=True)
    height = block_rows(gathered.shape[0])
    block_count = gathered.shape[0] // height
    blocks = gathered.reshape(block_count, height, gathered.shape[1])

    def one_block(current, block_item):
        class_block, offset = block_item
        scores = block_scores(class_block, offset * height)
        block_max = jnp.max(scores, axis=(0, 1))
        new_max = jnp.maximum(current[0], block_max)
        block_total = jnp.sum(jnp.exp(scores - new_max[None, None, :]), axis=(0, 1))
        return ((new_max, current[1] * jnp.exp(current[0] - new_max) + block_total), None)

    result, unused = lax.scan(
        one_block, initial, (blocks, jnp.arange(block_count, dtype=jnp.int32))
    )
    log_norm = result[0] + jnp.log(result[1])
    add_height = block_rows(gathered.shape[0])
    block_count = gathered.shape[0] // add_height
    blocks = gathered.reshape(block_count, add_height, gathered.shape[1])

    def one_block(current, block_item):
        class_block, offset = block_item
        row_start = offset * add_height
        scores = block_scores(class_block, row_start)
        responsibility = jnp.exp(scores - log_norm[None, None, :]).astype(jnp.bfloat16)
        spectra = jnp.einsum(
            "krb,pmr->pmkb", responsibility, turn_table, preferred_element_type=jnp.float32
        ).astype(jnp.bfloat16)
        products = jnp.einsum(
            "pmkb,mcb->kpmc", spectra, weighted, preferred_element_type=jnp.float32
        )
        real_sum = products[:, 0, :, :Q] + products[:, 1, :, Q:]
        imag_sum = products[:, 0, :, Q:] - products[:, 1, :, :Q]
        numerator = jnp.stack([real_sum, imag_sum], 2).reshape(add_height, 2 * M * Q)
        class_weight = jnp.sum(responsibility.astype(jnp.float32), axis=1)
        cycle_sum = jnp.dot(class_weight, power_term.T, precision=lax.Precision.HIGHEST)
        class_mass = jnp.sum(class_weight, axis=1)
        updated = (
            lax.dynamic_update_slice_in_dim(current[0], numerator, row_start, 0),
            lax.dynamic_update_slice_in_dim(current[1], cycle_sum, row_start, 0),
            lax.dynamic_update_slice_in_dim(current[2], class_mass, row_start, 0),
        )
        return (updated, None)

    result, unused = lax.scan(
        one_block, empty_sums, (blocks, jnp.arange(block_count, dtype=jnp.int32))
    )
    numer_all, cycles_all, mass_all = result
    merged = lax.psum((numer_all, cycles_all, mass_all), ("grp", "dev"))
    own_start = lax.axis_index("dev") * CLS_DEV
    numerator = lax.dynamic_slice_in_dim(merged[0], own_start, CLS_DEV, 0)
    cycle_sum = lax.dynamic_slice_in_dim(merged[1], own_start, CLS_DEV, 0)
    class_mass = lax.dynamic_slice_in_dim(merged[2], own_start, CLS_DEV, 0)
    new_references = (numerator.reshape(CLS_DEV, M, 2, Q) / cycle_sum[:, None, None, :]).reshape(
        CLS_DEV, 2 * M * Q
    )
    particle_total = columns * lax.axis_size("grp") * lax.axis_size("dev")
    occupancy = class_mass * (classes_total / particle_total)
    return (new_references, occupancy)


def solution(mesh):
    return jax.shard_map(
        local,
        mesh=mesh,
        in_specs=(P("dev", None), P(None, ("grp", "dev")), P(("grp", "dev")), P(), P(), P()),
        out_specs=(P("dev", None), P("dev")),
        check_vma=False,
    )
```

profile of v0, /device:TPU:2, one launch (start us, length us, event | category | flops | bytes accessed | tf_op | source)
XLA Modules:
  0.0 525.7 jit_solution(9444845568496355798)
XLA Ops:
  7.5 53.8 %all-gather = bf16[32,6,2048]{2,1,0:T(8,128)(2,1)S(1)} all-gather(bf16[1,6,2048]{2,1,0:T(8,128)(2,1)} %bitcast.179), channel_id=1, replica_groups=mesh['grp'=8,'dev'=32] {'dev'}, dimensions={0}, use_global_device_ids=true | all-gather | bytes 811008 | tf_op jit(solution)/shard_map/all_gather | solution.py:85
  61.2 1.2 reshape.224
  63.3 1.2 fusion.39
  64.5 87.8 %while.28 = (s32[]{:T(128)}, f32[256]{0:T(256)S(1)}, f32[256]{0:T(256)S(1)}, bf16[8,24,2048]{2,1,0:T(8,128)(2,1)}, bf16[32,64,256]{2,1,0:T(8,128)(2,1)}, /*index...) while((s32[]{:T(128)}, f32[256]{0:T(256)S(1)}, ...), condition=%wide.region_5.6_spmd.clone, body=%wide.region_0.5_spmd.clone.sunk | while | flops 159947328 | bytes 10727242 | solution.py:98
  67.3 2.5 fusion.111
  72.5 2.0 fusion.112
  78.3 2.5 fusion.111
  83.5 2.0 fusion.112
  89.2 2.5 fusion.111
  94.5 2.0 fusion.112
  100.2 2.5 fusion.111
  105.5 2.0 fusion.112
  111.2 2.5 fusion.111
  116.5 2.0 fusion.112
  122.2 2.5 fusion.111
  127.4 2.0 fusion.112
  133.2 2.5 fusion.111
  138.4 2.0 fusion.112
  144.2 2.5 fusion.111
  149.4 2.0 fusion.112
  152.6 106.6 %while.27 = (s32[]{:T(128)}, f32[192,2048]{1,0:T(8,128)S(1)}, f32[192,32]{1,0:T(8,128)S(1)}, f32[192]{0:T(256)S(1)}, bf16[8,24,2048]{2,1,0:T(8,128)(2,1)}, /*ind...) while((s32[]{:T(128)}, f32[192,2048]{1,0:T(8,128)S(1)}, ...), condition=%wide.region_11.12_spmd, body=%wide.region_6.11_spmd.sunk | while | flops 313785664 | bytes 12832803 | solution.py:130
  155.5 1.6 fusion.101
  159.9 1.3 convert_reduce_fusion.3
  161.6 2.0 convolution_bitcast_fusion.3
  168.9 1.6 fusion.101
  173.2 1.3 convert_reduce_fusion.3
  174.9 2.0 convolution_bitcast_fusion.3
  182.2 1.6 fusion.101
  186.6 1.3 convert_reduce_fusion.3
  188.2 2.0 convolution_bitcast_fusion.3
  195.5 1.6 fusion.101
  199.9 1.3 convert_reduce_fusion.3
  201.5 2.0 convolution_bitcast_fusion.3
  208.8 1.6 fusion.101
  213.2 1.3 convert_reduce_fusion.3
  214.9 2.0 convolution_bitcast_fusion.3
  222.1 1.6 fusion.101
  226.5 1.3 convert_reduce_fusion.3
  228.2 2.0 convolution_bitcast_fusion.3
  235.4 1.6 fusion.101
  239.8 1.3 convert_reduce_fusion.3
  241.5 2.0 convolution_bitcast_fusion.3
  248.7 1.6 fusion.101
  253.1 1.3 convert_reduce_fusion.3
  254.8 2.0 convolution_bitcast_fusion.3
  260.4 73.8 %all-reduce = (f32[192,32]{1,0:T(8,128)S(1)}, f32[192]{0:T(256)S(1)}) all-reduce(f32[192,32]{1,0:T(8,128)S(1)} %get-tuple-element.117, f32[192]{0:T(256)S(1)} %get-tuple-element.118), channel_id=1, replica_groups=mesh['grp'=8,'dev'=32] {'grp','dev'}, use_global_device_ids=true, to_apply=%region_13.14 | all-reduce | flops 6336 | bytes 50688 | tf_op jit(solution)/shard_map/psum | solution.py:134
  335.1 182.2 %all-reduce.3.cloned.1.call-done = f32[192,2048]{1,0:T(8,128)} async-done(((f32[192,2048]{1,0:T(8,128)}), f32[192,2048]{1,0:T(8,128)}) %all-reduce.3.cloned.1.call-update) | async-done | bytes 1572880 | tf_op jit(solution)/shard_map/psum | solution.py:134
  517.3 1.5 dynamic-slice_divide_fusion
  (325 shorter events, 111.0 us)
Async XLA Ops:
  7.2 55.2 %copy-start = (f32[64,32]{0,1:T(8,128)S(1)}, f32[64,32]{0,1:T(8,128)}, u32[]{:S(2)}) copy-start(f32[64,32]{0,1:T(8,128)} %param.13) | copy-start | bytes 24580
  7.2 56.1 %copy-start.2 = (bf16[2048,256]{1,0:T(8,128)(2,1)S(1)}, bf16[2048,256]{1,0:T(8,128)(2,1)}, u32[]{:S(2)}) copy-start(bf16[2048,256]{1,0:T(8,128)(2,1)} %param.11) | copy-start | bytes 3145732
  7.2 57.3 %copy-start.3 = (f32[192]{0:T(256)S(1)}, f32[192]{0:T(256)}, u32[]{:S(2)}) copy-start(f32[192]{0:T(256)} %param.15) | copy-start | bytes 2308
  7.2 510.1 %all-reduce.3.cloned.1.call-start = ((), (), s32[]{:S(2)}) async-start(), calls=%async_computation | async-start | bytes 3145728 | tf_op jit(solution)/shard_map/psum | solution.py:134
  259.2 1.1 copy-start.1
Sparse Core Ops, SparseCore 0:
  260.5 256.7 all-reduce.2
where the time goes:
time: 528 us; the launch traced here: 526 us
  waiting for transfers between devices  182 us (34%)
  blocking collectives  128 us (24%)
  matrix products  82.1 us (16%)
  local copies, waits for them, and re-layouts  64.7 us (12%)
  other arithmetic  42.8 us (8%)
  between operations  14.2 us (3%)
  loops' own time  12.1 us (2%)
    psum x1, waiting for transfers between devices, local(): merged = lax.psum((numer_all, cycles_all, mass_all), ('grp', 'dev'))  182 us
    psum x1, blocking collectives, local(): merged = lax.psum((numer_all, cycles_all, mass_all), ('grp', 'dev'))  73.8 us
    all_gather x1, blocking collectives, local(): gathered = lax.all_gather(references, 'dev', axis=0, tiled=True)  53.8 us
    dot_general x16, matrix products, block_scores(): jnp.einsum('pkmc,mcb->pmkb', stacked, weighted, preferred_element_type=jn...  32.7 us
    dot_general x16, matrix products, block_scores(): jnp.einsum('pmkb,pmr->krb', crossed, score_table, preferred_element_type=...  26.3 us
    dynamic_slice x32, local copies, waits for them, and re-layouts, local(): lax.scan(one_block, initial, (blocks, jnp.arange(block_count, dtype=jnp.i...  23.9 us
    reduce_sum x16, other arithmetic, class_rows(): jnp.sum(squares, axis=2) * factor[None, :, None]  18.6 us
    dot_general x8, matrix products, one_block(): jnp.einsum('pmkb,mcb->kpmc', spectra, weighted, preferred_element_type=jn...  15.7 us
  transfers between devices with their start and end apart: 1, of which 1 were waited for; matrix products, arithmetic and copies ran while one was open for 0% of the time, Pallas kernels for 0%

commit v1 on v0

--- a/solution.py
+++ b/solution.py
@@ -131,7 +131,8 @@
         one_block, empty_sums, (blocks, jnp.arange(block_count, dtype=jnp.int32))
     )
     numer_all, cycles_all, mass_all = result
-    merged = lax.psum((numer_all, cycles_all, mass_all), ("grp", "dev"))
+    partial = lax.psum((numer_all, cycles_all, mass_all), "dev")
+    merged = lax.psum(partial, "grp")
     own_start = lax.axis_index("dev") * CLS_DEV
     numerator = lax.dynamic_slice_in_dim(merged[0], own_start, CLS_DEV, 0)
     cycle_sum = lax.dynamic_slice_in_dim(merged[1], own_start, CLS_DEV, 0)

time: 528 us -> 585 us (1.11)
  blocking collectives: 128 us -> 216 us
  waiting for transfers between devices: 182 us -> 149 us
    psum x1 -> x2, blocking collectives: 73.8 us -> 163 us  [the longest x1 140 us: local(): partial = lax.psum((numer_all, cycles_all, mass_all), 'dev')]
    psum x1 -> x2, waiting for transfers between devices: 182 us -> 149 us  [the longest x1 149 us: local(): partial = lax.psum((numer_all, cycles_all, mass_all), 'dev')]
  transfers between devices with their start and end apart: 1 -> 2, of which waited for: 1 -> 1; matrix products, arithmetic and copies ran while one was open for 0% -> 0% of each run, Pallas kernels for 0% -> 0%
where the time goes in v1:
time: 585 us; the launch traced here: 581 us
  blocking collectives  216 us (37%)
  waiting for transfers between devices  149 us (25%)
  matrix products  82.1 us (14%)
  local copies, waits for them, and re-layouts  64.6 us (11%)
  other arithmetic  42.8 us (7%)
  between operations  14.2 us (2%)
  loops' own time  12.1 us (2%)
    psum x1, waiting for transfers between devices, local(): partial = lax.psum((numer_all, cycles_all, mass_all), 'dev')  149 us
    psum x1, blocking collectives, local(): partial = lax.psum((numer_all, cycles_all, mass_all), 'dev')  140 us
    all_gather x1, blocking collectives, local(): gathered = lax.all_gather(references, 'dev', axis=0, tiled=True)  53.8 us
    dot_general x16, matrix products, block_scores(): jnp.einsum('pkmc,mcb->pmkb', stacked, weighted, preferred_element_type=jn...  32.7 us
    dot_general x16, matrix products, block_scores(): jnp.einsum('pmkb,pmr->krb', crossed, score_table, preferred_element_type=...  26.3 us
    dynamic_slice x32, local copies, waits for them, and re-layouts, local(): lax.scan(one_block, initial, (blocks, jnp.arange(block_count, dtype=jnp.i...  23.9 us
    psum x1, blocking collectives, local(): merged = lax.psum(partial, 'grp')  22.2 us
    reduce_sum x16, other arithmetic, class_rows(): jnp.sum(squares, axis=2) * factor[None, :, None]  18.6 us
  transfers between devices with their start and end apart: 2, of which 1 were waited for; matrix products, arithmetic and copies ran while one was open for 0% of the time, Pallas kernels for 0%

profile of v1, /device:TPU:2, one launch (start us, length us, event | category | flops | bytes accessed | tf_op | source)
XLA Modules:
  0.0 581.2 jit_solution(14412001032394564507)
XLA Ops:
  7.5 53.8 %all-gather = bf16[32,6,2048]{2,1,0:T(8,128)(2,1)S(1)} all-gather(bf16[1,6,2048]{2,1,0:T(8,128)(2,1)} %bitcast.179), channel_id=1, replica_groups=mesh['grp'=8,'dev'=32] {'dev'}, dimensions={0}, use_global_device_ids=true | all-gather | bytes 811008 | tf_op jit(solution)/shard_map/all_gather | solution.py:85
  63.3 1.2 fusion.39
  64.5 87.8 %while.28 = (s32[]{:T(128)}, f32[256]{0:T(256)S(1)}, f32[256]{0:T(256)S(1)}, bf16[8,24,2048]{2,1,0:T(8,128)(2,1)}, bf16[32,64,256]{2,1,0:T(8,128)(2,1)}, /*index...) while((s32[]{:T(128)}, f32[256]{0:T(256)S(1)}, ...), condition=%wide.region_5.6_spmd.clone, body=%wide.region_0.5_spmd.clone.sunk | while | flops 159947328 | bytes 10727242 | solution.py:98
  67.3 2.5 fusion.111
  72.5 2.0 fusion.112
  78.3 2.5 fusion.111
  83.5 2.0 fusion.112
  89.2 2.5 fusion.111
  94.5 2.0 fusion.112
  100.2 2.5 fusion.111
  105.5 2.0 fusion.112
  111.2 2.5 fusion.111
  116.5 2.0 fusion.112
  122.2 2.5 fusion.111
  127.4 2.0 fusion.112
  133.2 2.5 fusion.111
  138.4 2.0 fusion.112
  144.2 2.5 fusion.111
  149.4 2.0 fusion.112
  152.6 106.6 %while.27 = (s32[]{:T(128)}, f32[192,2048]{1,0:T(8,128)S(1)}, f32[192,32]{1,0:T(8,128)S(1)}, f32[192]{0:T(256)S(1)}, bf16[8,24,2048]{2,1,0:T(8,128)(2,1)}, /*ind...) while((s32[]{:T(128)}, f32[192,2048]{1,0:T(8,128)S(1)}, ...), condition=%wide.region_11.12_spmd, body=%wide.region_6.11_spmd.sunk | while | flops 313785664 | bytes 12832803 | solution.py:130
  155.5 1.6 fusion.101
  159.9 1.3 convert_reduce_fusion.3
  161.6 2.0 convolution_bitcast_fusion.3
  168.9 1.6 fusion.101
  173.2 1.3 convert_reduce_fusion.3
  174.9 2.0 convolution_bitcast_fusion.3
  182.2 1.6 fusion.101
  186.6 1.3 convert_reduce_fusion.3
  188.2 2.0 convolution_bitcast_fusion.3
  195.5 1.6 fusion.101
  199.9 1.3 convert_reduce_fusion.3
  201.5 2.0 convolution_bitcast_fusion.3
  208.8 1.6 fusion.101
  213.2 1.3 convert_reduce_fusion.3
  214.9 2.0 convolution_bitcast_fusion.3
  222.1 1.6 fusion.101
  226.5 1.3 convert_reduce_fusion.3
  228.2 2.0 convolution_bitcast_fusion.3
  235.4 1.6 fusion.101
  239.8 1.3 convert_reduce_fusion.3
  241.5 2.0 convolution_bitcast_fusion.3
  248.7 1.6 fusion.101
  253.1 1.3 convert_reduce_fusion.3
  254.8 2.0 convolution_bitcast_fusion.3
  260.4 148.8 %all-reduce.5.cloned.1.call-done = f32[192,2048]{1,0:T(8,128)} async-done(((f32[192,2048]{1,0:T(8,128)}), f32[192,2048]{1,0:T(8,128)}) %all-reduce.5.cloned.1.call-update) | async-done | bytes 1572880 | tf_op jit(solution)/shard_map/psum | solution.py:134
  409.3 140.5 %all-reduce = (f32[192,32]{1,0:T(8,128)S(1)}, f32[192]{0:T(256)S(1)}) all-reduce(f32[192,32]{1,0:T(8,128)S(1)} %get-tuple-element.117, f32[192]{0:T(256)S(1)} %get-tuple-element.118), channel_id=1, replica_groups=mesh['grp'=8,'dev'=32] {'dev'}, use_global_device_ids=true, to_apply=%region_14.15 | all-reduce | flops 6336 | bytes 50688 | tf_op jit(solution)/shard_map/psum | solution.py:134
  549.7 22.2 %all-reduce.1 = (f32[192,32]{1,0:T(8,128)S(1)}, f32[192]{0:T(256)S(1)}) all-reduce(f32[192,32]{1,0:T(8,128)S(1)} %get-tuple-element.193, f32[192]{0:T(256)S(1)} %get-tuple-element.194), channel_id=1, replica_groups=mesh['grp'=8,'dev'=32] {'grp'}, use_global_device_ids=true, to_apply=%region_15.16 | all-reduce | flops 6336 | bytes 50688 | tf_op jit(solution)/shard_map/psum | solution.py:135
  572.9 1.5 dynamic-slice_divide_fusion
  (329 shorter events, 112.2 us)
Async XLA Ops:
  7.2 55.2 %copy-start = (f32[64,32]{0,1:T(8,128)S(1)}, f32[64,32]{0,1:T(8,128)}, u32[]{:S(2)}) copy-start(f32[64,32]{0,1:T(8,128)} %param.13) | copy-start | bytes 24580
  7.2 56.1 %copy-start.2 = (bf16[2048,256]{1,0:T(8,128)(2,1)S(1)}, bf16[2048,256]{1,0:T(8,128)(2,1)}, u32[]{:S(2)}) copy-start(bf16[2048,256]{1,0:T(8,128)(2,1)} %param.11) | copy-start | bytes 3145732
  7.2 57.3 %copy-start.3 = (f32[192]{0:T(256)S(1)}, f32[192]{0:T(256)}, u32[]{:S(2)}) copy-start(f32[192]{0:T(256)} %param.15) | copy-start | bytes 2308
  7.2 402.0 %all-reduce.5.cloned.1.call-start = ((), (), s32[]{:S(2)}) async-start(), calls=%async_computation | async-start | bytes 3145728 | tf_op jit(solution)/shard_map/psum | solution.py:134
  259.2 1.1 copy-start.1
  260.4 312.5 %all-reduce.7.cloned.1.call-start = ((), (), s32[]{:S(2)}) async-start(), calls=%async_computation.1 | async-start | bytes 3145728 | tf_op jit(solution)/shard_map/psum | solution.py:135
Sparse Core Ops, SparseCore 0:
  260.5 148.6 all-reduce.4
  411.7 63.9 all-reduce.6
